TPU v7x, 32 devices: a whole 2x2x4 slice. The times are simulated.
32 devices in a mesh: dp: 4 (over y, x), expert: 8 (over z, core).
Axes of the slice: x: 2, y: 2, z: 4, core: 2. Of those that a mesh axis runs over, the one named last changes fastest.
Arguments:
- tokens: bfloat16 [8, 512, 2048], P('expert', 'dp'), may hold values from -6 to 6
- segment_ids: int32 [8, 512], P('expert', 'dp'), may hold values from 0 to 2, never falling along the last dimension, each value on 1 to 256 neighbouring positions
- routes: int32 [8, 512, 6], P('expert', 'dp'), may hold values from 0 to 15, all different within a row; in each aligned block of 128 rows (0 to 127, 128 to 255, ..., all dimensions but the last counted through in order) at most 64 rows name the same one
- norm_gain: float32 [2048], replicated, may hold values from 0.25 to 1.75
- w_query: bfloat16 [2048, 2048], P(None, 'dp')
- w_key: bfloat16 [2048, 512], P(None, 'dp')
- w_value: bfloat16 [2048, 512], P(None, 'dp'), may hold values from -0.125 to 0.125
- w_out: bfloat16 [2048, 2048], P('dp'), may hold values from -0.125 to 0.125
- ffn_gain: float32 [2048], replicated, may hold values from 0.25 to 1.75
- w_router: bfloat16 [2048, 16], replicated, may hold values from -0.125 to 0.125
- w_shared_gate: bfloat16 [2048, 2816], P(None, 'dp'), may hold values from -0.125 to 0.125
- w_shared_up: bfloat16 [2048, 2816], P(None, 'dp'), may hold values from -0.125 to 0.125
- w_shared_down: bfloat16 [2816, 2048], P('dp'), may hold values from -0.109375 to 0.109375
- w_expert_gate: bfloat16 [2048, 22528], P(None, ('dp', 'expert')), may hold values from -0.125 to 0.125
- w_expert_up: bfloat16 [2048, 22528], P(None, ('dp', 'expert')), may hold values from -0.125 to 0.125
- w_expert_down: bfloat16 [22528, 2048], P(('dp', 'expert')), may hold values from -0.15625 to 0.15625
Outputs:
- layer_out: bfloat16 [8, 512, 2048], P('expert', 'dp')
Inputs may be any that keep to these rules, and one draw needn't show every extreme that they name: `routes`: each row names 6 different experts. In each aligned block of 128 rows (stream-major order; the rows of one device) no expert is named more than 64 times, a bound that some block reaches. `segment_ids`: along each stream ids never fall; each of the 3 prompts covers 1 to 256 tokens, one exactly 256.
All inputs are finite; a program needn't handle non-finite values.
Results may differ from a plain program's by a relative error of at most 0.02.
The roundings to bfloat16 on the way count: a program that leaves them out, or rounds other values in their place, can miss the bound.
Values may be sent and summed in bfloat16 or wider, within the bound.
No kernel may reach another device: no remote copies, remote signals or barrier semaphores. Data moves between devices by JAX's collectives and lax.ppermute only.
A program may use at most 128 MiB of HBM per device.

v0:
```python
import jax
import jax.numpy as jnp
from jax import lax
from jax.sharding import PartitionSpec as P

HD = 128
TOP = 6


epsilon = 1e-06


def rms_norm(values, gain):
    wide = values.astype(jnp.float32)
    scale = lax.rsqrt(jnp.mean(wide * wide, axis=-1, keepdims=True) + epsilon)
    return (wide * scale * gain).astype(jnp.bfloat16)


def positions(segment):
    count = segment.shape[0]
    index = jnp.arange(count, dtype=jnp.int32)
    same = (segment[:, None] == segment[None, :]) & (index[None, :] < index[:, None])
    return jnp.sum(same.astype(jnp.int32), axis=1)


def rotate(heads, place):
    half = heads.shape[-1] // 2
    freq = 10000.0 ** (-jnp.arange(half, dtype=jnp.float32) / half)
    angle = place.astype(jnp.float32)[:, None] * freq[None, :]
    cosine = jnp.cos(angle)[:, None, :]
    sine = jnp.sin(angle)[:, None, :]
    first = heads[..., :half]
    second = heads[..., half:]
    return jnp.concatenate(
        [first * cosine - second * sine, second * cosine + first * sine], axis=-1
    )


def attend(normed, segment, w_query, w_key, w_value):
    rows = normed.shape[0]
    query_heads = w_query.shape[1] // HD
    value_heads = w_key.shape[1] // HD
    group_size = query_heads // value_heads
    place = positions(segment)
    query = jnp.dot(normed, w_query, preferred_element_type=jnp.float32).reshape(
        rows, query_heads, HD
    )
    query = rotate(query, place).astype(jnp.bfloat16).reshape(rows, value_heads, group_size, HD)
    keyed = jnp.dot(normed, w_key, preferred_element_type=jnp.float32).reshape(
        rows, value_heads, HD
    )
    keyed = rotate(keyed, place).astype(jnp.bfloat16)
    valued = (
        jnp.dot(normed, w_value, preferred_element_type=jnp.float32)
        .astype(jnp.bfloat16)
        .reshape(rows, value_heads, HD)
    )
    block = min(rows, 512)
    index = jnp.arange(rows, dtype=jnp.int32)

    def one_block(start):
        index_block = start + jnp.arange(block, dtype=jnp.int32)
        scores = jnp.einsum(
            "qkgd,skd->kgqs", query, keyed, preferred_element_type=jnp.float32
        ) * HD ** (-0.5)
        allowed = (segment[:, None] == segment[None, :]) & (index[None, :] <= index_block[:, None])
        scores = jnp.where(allowed[None, None], scores, -1e30)
        highest = jnp.max(scores, axis=-1, keepdims=True)
        expo = jnp.exp(scores - highest)
        weights = (expo / jnp.sum(expo, axis=-1, keepdims=True)).astype(jnp.bfloat16)
        mixed = jnp.einsum("kgqs,skd->qkgd", weights, valued, preferred_element_type=jnp.float32)
        return mixed.astype(jnp.bfloat16).reshape(block, query_heads * HD)

    starts = jnp.arange(rows // block, dtype=jnp.int32) * block
    return lax.map(one_block, starts).reshape(rows, query_heads * HD)


def expert_rows(rows, w_expert_gate, w_expert_up, w_expert_down):
    shape = rows.shape
    flat = rows.reshape(-1, shape[-1])
    gated = jnp.dot(flat, w_expert_gate, preferred_element_type=jnp.float32)
    lifted = jnp.dot(flat, w_expert_up, preferred_element_type=jnp.float32)
    active = (jax.nn.silu(gated) * lifted).astype(jnp.bfloat16)
    return (
        jnp.dot(active, w_expert_down, preferred_element_type=jnp.float32)
        .astype(jnp.bfloat16)
        .reshape(shape)
    )


def per_device(
    tokens,
    segment_ids,
    routes,
    norm_gain,
    w_query,
    w_key,
    w_value,
    w_out,
    ffn_gain,
    w_router,
    w_shared_gate,
    w_shared_up,
    w_shared_down,
    w_expert_gate,
    w_expert_up,
    w_expert_down,
):
    own_rows = tokens[0]
    tok_count = own_rows.shape[0]
    width = own_rows.shape[1]
    normed = rms_norm(own_rows, norm_gain)
    group_rows, group_segments = (
        lax.all_gather(normed, "dp", axis=0, tiled=True),
        lax.all_gather(segment_ids[0], "dp", axis=0, tiled=True),
    )
    attended = attend(group_rows, group_segments, w_query, w_key, w_value)
    head_sum = lax.psum_scatter(
        jnp.dot(attended, w_out, preferred_element_type=jnp.float32).astype(jnp.bfloat16),
        "dp",
        scatter_dimension=0,
        tiled=True,
    ).astype(jnp.float32)
    residual = (own_rows.astype(jnp.float32) + head_sum).astype(jnp.bfloat16)
    mixed = rms_norm(residual, ffn_gain)
    piece = lax.all_gather(mixed, "dp", axis=0, tiled=True)
    gated = jnp.dot(piece, w_shared_gate, preferred_element_type=jnp.float32)
    lifted = jnp.dot(piece, w_shared_up, preferred_element_type=jnp.float32)
    hidden = (jax.nn.silu(gated) * lifted).astype(jnp.bfloat16)
    shared_sum = lax.psum_scatter(
        jnp.dot(hidden, w_shared_down, preferred_element_type=jnp.float32).astype(jnp.bfloat16),
        "dp",
        scatter_dimension=0,
        tiled=True,
    ).astype(jnp.float32)
    expert_count = w_router.shape[1]
    capacity = 4 * tok_count * TOP // (3 * expert_count)
    own_routes = routes[0]
    route_flat = own_routes.reshape(-1)
    labels = jnp.arange(expert_count, dtype=jnp.int32)
    onehot = (route_flat[:, None] == labels[None, :]).astype(jnp.int32)
    slot = jnp.sum(jnp.cumsum(onehot, axis=0) * onehot, axis=1) - 1
    target = route_flat * capacity + slot
    placed = target[:, None] == jnp.arange(expert_count * capacity, dtype=jnp.int32)[None, :]
    placed = jnp.any(placed.reshape(tok_count, TOP, expert_count * capacity), axis=1).astype(
        jnp.bfloat16
    )
    send = lax.dot_general(
        placed, mixed, (((0,), (0,)), ((), ())), preferred_element_type=jnp.float32
    ).astype(jnp.bfloat16)
    logits = jnp.dot(mixed, w_router, preferred_element_type=jnp.float32)
    chosen = jnp.sum(
        jnp.where(own_routes[:, :, None] == labels[None, None, :], logits[:, None, :], 0.0), axis=2
    )
    highest = jnp.max(chosen, axis=1, keepdims=True)
    expo = jnp.exp(chosen - highest)
    gates = expo / jnp.sum(expo, axis=1, keepdims=True)
    doubled = jnp.repeat(send.reshape(expert_count, capacity, width), 2, axis=0)
    partial_rows = expert_rows(
        lax.all_to_all(doubled, ("dp", "expert"), split_axis=0, concat_axis=0, tiled=True),
        w_expert_gate,
        w_expert_up,
        w_expert_down,
    )
    returned = lax.all_to_all(
        partial_rows, ("dp", "expert"), split_axis=0, concat_axis=0, tiled=True
    )
    returned = returned.astype(jnp.float32).reshape(expert_count, 2, capacity, width)
    result_rows = (
        (returned[:, 0] + returned[:, 1])
        .astype(jnp.bfloat16)
        .reshape(expert_count * capacity, width)
    )
    picked = result_rows[target].reshape(tok_count, TOP, width).astype(jnp.float32)
    routed = jnp.sum(gates[:, :, None] * picked, axis=1)
    output = (residual.astype(jnp.float32) + shared_sum + routed).astype(jnp.bfloat16)
    return output[None]


def solution(mesh):
    in_specs = (
        P("expert", "dp", None),
        P("expert", "dp"),
        P("expert", "dp", None),
        P(),
        P(None, "dp"),
        P(None, "dp"),
        P(None, "dp"),
        P("dp", None),
        P(),
        P(),
        P(None, "dp"),
        P(None, "dp"),
        P("dp", None),
        P(None, ("dp", "expert")),
        P(None, ("dp", "expert")),
        P(("dp", "expert"), None),
    )
    out_specs = P("expert", "dp", None)
    return jax.shard_map(
        per_device, mesh=mesh, in_specs=in_specs, out_specs=out_specs, check_vma=False
    )
```

profile of v0, /device:TPU:0, one launch (start us, length us, event | category | flops | bytes accessed | tf_op | source)
XLA Modules:
  0.0 586.5 jit_solution(2181251678079823622)
XLA Ops:
  6.5 1.4 fusion.19
  7.9 2.0 fusion.21
  10.0 9.5 %all-gather = s32[1,512]{1,0:T(1,128)S(1)} all-gather(s32[1,128]{1,0:T(1,128)} %param.17), channel_id=2, replica_groups=mesh['dp'=4,'expert'=8] {'dp'}, dimensions={1}, use_global_device_ids=true | all-gather | bytes 2560 | tf_op jit(solution)/shard_map/all_gather | solution.py:115
  20.0 1.8 multiply_cosine_fusion
  21.7 26.3 %all-gather.4.cloned.1.call-done = bf16[512,2048]{1,0:T(8,128)(2,1)} async-done(((bf16[128,2048]{1,0:T(8,128)(2,1)}), bf16[512,2048]{1,0:T(8,128)(2,1)}) %all-gather.4.cloned.1.call-update) | async-done | bytes 2097168 | tf_op jit(solution)/shard_map/all_gather | solution.py:114
  48.0 3.5 fusion.53
  52.7 2.4 copy.59
  55.0 2.4 copy.60
  57.5 2.6 convolution_bitcast_fusion
  62.2 1.9 copy-done.2
  65.0 5.9 %fusion.10 = bf16[128,4,512]{2,0,1:T(8,128)(2,1)} fusion(f32[4,512]{1,0:T(4,128)S(1)} %fusion.2, f32[4,512]{1,0:T(4,128)S(1)} %get-tuple-element.34, f32[512,512,4]{1,0,2:T(8,128)} %copy-done.2, pred[512,512]{0,1:T(8,128)(4,1)S(1)} %compare_and_fusion.1, bf16[512,2048]{1,0:T(8,128)(2,1)} %all-gather.4.cloned.1.call-done, bf16[2048,128]{1,0:T(8,128)(2,1)} %param.22), kind=kOutput, calls=%fused_computation.32 | convolution fusion | flops 542441472 | bytes 7618560 | tf_op jit(solution)/shard_map/while/body/eval_jaxpr/kgqs,skd->qkgd/dot_general | solution.py:71
  70.9 4.4 convolution_convert_fusion.3
  76.4 3.2 reduce-window.6
  82.2 28.5 %reduce-scatter.3.cloned.1.call-done = bf16[128,2048]{1,0:T(8,128)(2,1)} async-done(((bf16[512,2048]{1,0:T(8,128)(2,1)}), bf16[128,2048]{1,0:T(8,128)(2,1)}) %reduce-scatter.3.cloned.1.call-update) | async-done | bytes 524304 | tf_op jit(solution)/shard_map/reduce_scatter | solution.py:118
  112.0 2.1 fusion.16
  114.1 4.3 convolution_convert_fusion.1
  118.4 6.8 %broadcast_in_dim.49 = bf16[16,2,64,2048]{3,2,1,0:T(8,128)(2,1)} broadcast(bf16[16,64,2048]{2,1,0:T(8,128)(2,1)} %bitcast.119), dimensions={0,2,3} | broadcast | bytes 12582912 | tf_op jit(solution)/shard_map/broadcast_in_dim | solution.py:158
  125.2 189.4 %all_to_all.10 = bf16[32,64,2048]{2,1,0:T(8,128)(2,1)S(1)} all-to-all(bf16[32,64,2048]{2,1,0:T(8,128)(2,1)} %bitcast.118), channel_id=1, replica_groups=mesh['dp'=4,'expert'=8] {'dp','expert'}, dimensions={0} | all-to-all | bytes 16777216 | tf_op jit(solution)/shard_map/all_to_all | solution.py:160
  314.5 3.2 copy-done.5
  317.8 8.0 %fusion.56 = f32[2048,704]{0,1:T(8,128)} fusion(bf16[2048,2048]{1,0:T(8,128)(2,1)S(1)} %bitcast.121, bf16[2048,704]{0,1:T(8,128)(2,1)S(1)} %copy-done.11), kind=kOutput, calls=%fused_computation.105 | convolution fusion | flops 5905580032 | bytes 17039360 | tf_op jit(solution)/shard_map/dot_general | solution.py:81
  325.7 19.1 %convolution_convert_fusion = bf16[2048,2048]{1,0:T(8,128)(2,1)} fusion(bf16[704,2048]{1,0:T(8,128)(2,1)S(1)} %copy-done, f32[2048,704]{0,1:T(8,128)} %fusion.56, bf16[2048,2048]{1,0:T(8,128)(2,1)} %bitcast.122, bf16[2048,704]{0,1:T(8,128)(2,1)} %param.30), kind=kOutput, calls=%fused_computation.6 | convolution fusion | flops 11824005120 | bytes 28311552 | tf_op jit(solution)/shard_map/dot_general | solution.py:85
  344.8 3.9 all-to-all-start.1
  349.7 84.7 %all-gather.6.cloned.1.call-done = bf16[512,2048]{1,0:T(8,128)(2,1)} async-done(((bf16[128,2048]{1,0:T(8,128)(2,1)}), bf16[512,2048]{1,0:T(8,128)(2,1)}) %all-gather.6.cloned.1.call-update) | async-done | bytes 2097168 | tf_op jit(solution)/shard_map/all_gather | solution.py:126
  434.4 4.4 fusion.54
  438.8 8.6 %convolution_convert_fusion.2 = bf16[512,2048]{1,0:T(8,128)(2,1)} fusion(bf16[704,2048]{1,0:T(8,128)(2,1)} %param.28, bf16[512,2048]{1,0:T(8,128)(2,1)} %all-gather.6.cloned.1.call-done, bf16[2048,704]{0,1:T(8,128)(2,1)} %param.27, f32[512,704]{0,1:T(8,128)} %fusion.54), kind=kOutput, calls=%fused_computation.16 | convolution fusion | flops 2956001280 | bytes 11403264 | tf_op jit(solution)/shard_map/dot_general | solution.py:131
  448.2 85.3 %all-to-all-done.1 = bf16[32,64,2048]{2,1,0:T(8,128)(2,1)} async-done(((bf16[32,64,2048]{2,1,0:T(8,128)(2,1)}), bf16[32,64,2048]{2,1,0:T(8,128)(2,1)}, u32[]{:S(2)}, u32[]{:S(2)}) %all-to-all-start.1) | async-done | bytes 8388640 | tf_op jit(solution)/shard_map/all_to_all | solution.py:165
  533.5 11.2 %convert.22 = f32[16,2,64,2048]{3,2,1,0:T(8,128)} convert(bf16[16,2,64,2048]{3,2,1,0:T(8,128)(2,1)} %bitcast.23) | non-fusion elementwise | flops 4194304 | bytes 25165824 | tf_op jit(solution)/shard_map/reshape | solution.py:168
  544.7 8.5 %fusion.1 = bf16[16,1,64,2048]{3,2,0,1:T(8,128)(2,1)} fusion(f32[16,2,64,2048]{3,2,1,0:T(8,128)} %convert.22), kind=kLoop, calls=%fused_computation.3 | loop fusion | flops 4194304 | bytes 20971520 | tf_op jit(solution)/shard_map/convert_element_type | solution.py:171
  553.3 9.8 %gather_fusion = bf16[768,2048]{1,0:T(8,128)(2,1)} fusion(bf16[1024,2048]{1,0:T(8,128)(2,1)} %bitcast.117, s32[1024]{0:T(1024)S(1)} %pad_clamp_fusion), kind=kCustom, calls=%fused_computation | custom fusion | bytes 6294528 | tf_op jit(solution)/shard_map/gather | solution.py:174
  563.1 6.6 %reshape.369 = f32[128,6,2048]{2,1,0:T(8,128)} reshape(bf16[768,2048]{1,0:T(8,128)(2,1)} %gather_fusion) | data formatting | bytes 9437184 | tf_op jit(solution)/shard_map/convert_element_type | solution.py:174
  569.6 7.8 %multiply_reduce_fusion = f32[128,2048]{1,0:T(8,128)} fusion(f32[128,6,2048]{2,1,0:T(8,128)} %reshape.369, f32[128,6]{1,0:T(8,128)S(1)} %copy.45), kind=kLoop, calls=%fused_computation.5 | loop fusion | flops 2883584 | bytes 7343104 | tf_op jit(solution)/shard_map/reduce_sum | solution.py:175
  577.4 2.6 fusion.23
  (69 shorter events, 11.2 us)
Async XLA Ops:
  6.5 319.2 %copy-start = (bf16[704,2048]{1,0:T(8,128)(2,1)S(1)}, bf16[704,2048]{1,0:T(8,128)(2,1)}, u32[]{:S(2)}) copy-start(bf16[704,2048]{1,0:T(8,128)(2,1)} %param.31) | copy-start | bytes 8650756
  6.5 41.5 %all-gather.4.cloned.1.call-start = ((), (), s32[]{:S(2)}) async-start(), calls=%async_computation.4 | async-start | bytes 2621440 | tf_op jit(solution)/shard_map/all_gather | solution.py:114
  10.0 100.8 %reduce-scatter.3.cloned.1.call-start = ((), (), s32[]{:S(2)}) async-start(), calls=%async_computation.5 | async-start | bytes 2621440 | tf_op jit(solution)/shard_map/reduce_scatter | solution.py:118
  57.4 3.2 copy-start.6
  57.4 3.2 copy-start.7
  57.5 3.2 copy-start.8
  62.2 1.9 copy-start.2
  70.9 4.5 copy-start.10
  70.9 39.8 %copy-start.3 = (bf16[1,128,2048]{2,1,0:T(8,128)(2,1)S(1)}, bf16[1,128,2048]{2,1,0:T(8,128)(2,1)}, u32[]{:S(2)}) copy-start(bf16[1,128,2048]{2,1,0:T(8,128)(2,1)} %param.16) | copy-start | bytes 1572868
  125.2 192.6 %copy-start.11 = (bf16[2048,704]{0,1:T(8,128)(2,1)S(1)}, bf16[2048,704]{0,1:T(8,128)(2,1)}, u32[]{:S(2)}) copy-start(bf16[2048,704]{0,1:T(8,128)(2,1)} %param.29) | copy-start | bytes 8650756
  314.5 3.2 copy-start.5
  344.8 89.6 %copy-start.12 = (bf16[2048,704]{0,1:T(8,128)(2,1)S(1)}, bf16[2048,704]{0,1:T(8,128)(2,1)}, u32[]{:S(2)}) copy-start(bf16[2048,704]{0,1:T(8,128)(2,1)} %param.26) | copy-start | bytes 8650756
  344.8 188.7 %all-to-all-start.1 = ((bf16[32,64,2048]{2,1,0:T(8,128)(2,1)}), bf16[32,64,2048]{2,1,0:T(8,128)(2,1)}, u32[]{:S(2)}, u32[]{:S(2)}) async-start(bf16[32,64,2048]{2,1,0:T(8,128)(2,1)} %bitcast.120), calls=%async_computation.3 | async-start | bytes 16777216 | tf_op jit(solution)/shard_map/all_to_all | solution.py:165
  348.7 85.7 %all-gather.6.cloned.1.call-start = ((), (), s32[]{:S(2)}) async-start(), calls=%async_computation.6 | async-start | bytes 2621440 | tf_op jit(solution)/shard_map/all_gather | solution.py:126
  349.5 228.0 %reduce-scatter.5.cloned.1.call-start = ((), (), s32[]{:S(2)}) async-start(), calls=%async_computation.7 | async-start | bytes 2621440 | tf_op jit(solution)/shard_map/reduce_scatter | solution.py:130
  438.8 9.0 %copy-start.4 = (bf16[128,2048]{1,0:T(8,128)(2,1)S(1)}, bf16[128,2048]{1,0:T(8,128)(2,1)}, u32[]{:S(2)}) copy-start(bf16[128,2048]{1,0:T(8,128)(2,1)} %fusion.16) | copy-start | bytes 1572868
  438.8 9.0 %copy-start.9 = (bf16[2048,16]{0,1:T(8,128)(2,1)S(1)}, bf16[2048,16]{0,1:T(8,128)(2,1)}, u32[]{:S(2)}) copy-start(bf16[2048,16]{0,1:T(8,128)(2,1)} %param.25) | copy-start | bytes 196612
  569.6 10.4 %copy-start.1 = (bf16[704,2048]{1,0:T(8,128)(2,1)S(1)}, bf16[704,2048]{1,0:T(8,128)(2,1)}, u32[]{:S(2)}) copy-start(bf16[704,2048]{1,0:T(8,128)(2,1)} %param.31) | copy-start | bytes 8650756
Sparse Core Ops, SparseCore 0:
  10.1 37.8 all-gather.3
  75.5 35.1 reduce-scatter.2
  351.4 82.9 all-gather.5
  447.5 60.0 reduce-scatter.4
where the time goes:
time: 587 us
  waiting for transfers between devices  226 us (39%)
  blocking collectives  199 us (34%)
  matrix products  62.3 us (11%)
  other arithmetic  46.2 us (8%)
  local copies, waits for them, and re-layouts  36 us (6%)
  between operations  13.3 us (2%)
    all_to_all x1, blocking collectives, per_device(): lax.all_to_all(doubled, ('dp', 'expert'), split_axis=0, concat_axis=0, ti...  189 us
    all_to_all x1, waiting for transfers between devices, per_device(): lax.all_to_all(partial_rows, ('dp', 'expert'), split_axis=0, concat_axis=...  85.3 us
    all_gather x1, waiting for transfers between devices, per_device(): piece = lax.all_gather(mixed, 'dp', axis=0, tiled=True)  84.7 us
    reduce_scatter x1, waiting for transfers between devices, per_device(): lax.psum_scatter(jnp.dot(attended, w_out, preferred_element_type=jnp.floa...  28.5 us
    all_gather x1, waiting for transfers between devices, per_device(): lax.all_gather(normed, 'dp', axis=0, tiled=True)  26.3 us
    dot_general x1, matrix products, expert_rows(): jnp.dot(active, w_expert_down, preferred_element_type=jnp.float32)  19.1 us
  transfers between devices with their start and end apart: 5, of which 4 were waited for; matrix products, arithmetic and copies ran while one was open for 11% of the time, Pallas kernels for 0%

commit v1 on v0

--- a/solution.py
+++ b/solution.py
@@ -134,54 +134,74 @@
         tiled=True,
     ).astype(jnp.float32)
     expert_count = w_router.shape[1]
+    dp_size = lax.axis_size("dp")
+    planes = lax.axis_size("zc")
+    plane = lax.axis_index("zc")
     capacity = 4 * tok_count * TOP // (3 * expert_count)
-    own_routes = routes[0]
-    route_flat = own_routes.reshape(-1)
+    depth = planes * capacity
+    slots = dp_size * depth
+    mixed_g = lax.all_gather(mixed, "zc", axis=0, tiled=True)
+    routes_g = lax.all_gather(routes[0], "zc", axis=0, tiled=True)
+    rows_g = mixed_g.shape[0]
     labels = jnp.arange(expert_count, dtype=jnp.int32)
-    onehot = (route_flat[:, None] == labels[None, :]).astype(jnp.int32)
-    slot = jnp.sum(jnp.cumsum(onehot, axis=0) * onehot, axis=1) - 1
-    target = route_flat * capacity + slot
-    placed = target[:, None] == jnp.arange(expert_count * capacity, dtype=jnp.int32)[None, :]
-    placed = jnp.any(placed.reshape(tok_count, TOP, expert_count * capacity), axis=1).astype(
-        jnp.bfloat16
-    )
-    send = lax.dot_general(
-        placed, mixed, (((0,), (0,)), ((), ())), preferred_element_type=jnp.float32
-    ).astype(jnp.bfloat16)
-    logits = jnp.dot(mixed, w_router, preferred_element_type=jnp.float32)
+    logits = jnp.dot(mixed_g, w_router, preferred_element_type=jnp.float32)
     chosen = jnp.sum(
-        jnp.where(own_routes[:, :, None] == labels[None, None, :], logits[:, None, :], 0.0), axis=2
+        jnp.where(routes_g[:, :, None] == labels[None, None, :], logits[:, None, :], 0.0), axis=2
     )
     highest = jnp.max(chosen, axis=1, keepdims=True)
     expo = jnp.exp(chosen - highest)
     gates = expo / jnp.sum(expo, axis=1, keepdims=True)
-    doubled = jnp.repeat(send.reshape(expert_count, capacity, width), 2, axis=0)
-    partial_rows = expert_rows(
-        lax.all_to_all(doubled, ("dp", "expert"), split_axis=0, concat_axis=0, tiled=True),
-        w_expert_gate,
-        w_expert_up,
-        w_expert_down,
-    )
-    returned = lax.all_to_all(
-        partial_rows, ("dp", "expert"), split_axis=0, concat_axis=0, tiled=True
-    )
-    returned = returned.astype(jnp.float32).reshape(expert_count, 2, capacity, width)
-    result_rows = (
-        (returned[:, 0] + returned[:, 1])
-        .astype(jnp.bfloat16)
-        .reshape(expert_count * capacity, width)
-    )
-    picked = result_rows[target].reshape(tok_count, TOP, width).astype(jnp.float32)
-    routed = jnp.sum(gates[:, :, None] * picked, axis=1)
+    route_flat = routes_g.reshape(-1)
+    inside = (route_flat % planes) == plane
+    dest = route_flat // planes
+    onehot = ((dest[:, None] == jnp.arange(dp_size, dtype=jnp.int32)[None, :]) & inside[:, None]).astype(jnp.int32)
+    slot = jnp.sum(jnp.cumsum(onehot, axis=0) * onehot, axis=1) - 1
+    target = jnp.where(inside, dest * depth + slot, -1).reshape(rows_g, TOP)
+    hit = target[:, :, None] == jnp.arange(slots, dtype=jnp.int32)[None, None, :]
+    placed = jnp.any(hit, axis=1).astype(jnp.bfloat16)
+    send = lax.dot_general(
+        placed, mixed_g, (((0,), (0,)), ((), ())), preferred_element_type=jnp.float32
+    ).astype(jnp.bfloat16)
+    recv = lax.all_to_all(send.reshape(dp_size, depth, width), "dp", 0, 0, tiled=True)
+    mine = recv.reshape(slots, width)
+    swap = [(0, 1), (1, 0)]
+    other = lax.ppermute(mine, "core", swap)
+    half_rows = expert_rows(
+        jnp.concatenate([mine, other], axis=0), w_expert_gate, w_expert_up, w_expert_down
+    )
+    from_partner = lax.ppermute(half_rows[slots:], "core", swap)
+    expert_out = (
+        half_rows[:slots].astype(jnp.float32) + from_partner.astype(jnp.float32)
+    ).astype(jnp.bfloat16)
+    back = lax.all_to_all(
+        expert_out.reshape(dp_size, depth, width), "dp", 0, 0, tiled=True
+    ).reshape(slots, width)
+    comb = jnp.sum(jnp.where(hit, gates[:, :, None], 0.0), axis=1)
+    first = comb.astype(jnp.bfloat16)
+    rest = comb - first.astype(jnp.float32)
+    second = rest.astype(jnp.bfloat16)
+    third = (rest - second.astype(jnp.float32)).astype(jnp.bfloat16)
+    partial = (
+        jnp.dot(first, back, preferred_element_type=jnp.float32)
+        + jnp.dot(second, back, preferred_element_type=jnp.float32)
+        + jnp.dot(third, back, preferred_element_type=jnp.float32)
+    )
+    routed = lax.psum_scatter(
+        partial.astype(jnp.bfloat16), "zc", scatter_dimension=0, tiled=True
+    ).astype(jnp.float32)
     output = (residual.astype(jnp.float32) + shared_sum + routed).astype(jnp.bfloat16)
     return output[None]
 
 
 def solution(mesh):
+    dp_size = mesh.shape["dp"]
+    planes = mesh.shape["expert"] // 2
+    fine = jax.sharding.Mesh(mesh.devices.reshape(dp_size, planes, 2), ("dp", "zc", "core"))
+    ex = ("zc", "core")
     in_specs = (
-        P("expert", "dp", None),
-        P("expert", "dp"),
-        P("expert", "dp", None),
+        P(ex, "dp", None),
+        P(ex, "dp"),
+        P(ex, "dp", None),
         P(),
         P(None, "dp"),
         P(None, "dp"),
@@ -192,11 +212,11 @@
         P(None, "dp"),
         P(None, "dp"),
         P("dp", None),
-        P(None, ("dp", "expert")),
-        P(None, ("dp", "expert")),
-        P(("dp", "expert"), None),
-    )
-    out_specs = P("expert", "dp", None)
+        P(None, ("dp",) + ex),
+        P(None, ("dp",) + ex),
+        P(("dp",) + ex, None),
+    )
+    out_specs = P(ex, "dp", None)
     return jax.shard_map(
-        per_device, mesh=mesh, in_specs=in_specs, out_specs=out_specs, check_vma=False
-    )
+        per_device, mesh=fine, in_specs=in_specs, out_specs=out_specs, check_vma=False
+    )

time: 587 us -> 441 us (0.75); the launches traced: 587 us -> 434 us
  blocking collectives: 199 us -> 88.4 us
  waiting for transfers between devices: 226 us -> 194 us
  matrix products: 62.3 us -> 82.1 us
  local copies, waits for them, and re-layouts: 36 us -> 19.2 us
  other arithmetic: 46.2 us -> 30.5 us
    all_to_all x1, blocking collectives: 189 us -> 51.4 us  [per_device(): lax.all_to_all(send.reshape(dp_size, depth, width), 'dp', 0, 0, tiled=True)]
    all_to_all x1, waiting for transfers between devices: 85.3 us -> 0.01 us  [per_device(): lax.all_to_all(expert_out.reshape(dp_size, depth, width), 'dp', 0, 0, til...]
    reduce_scatter x0 -> x1, waiting for transfers between devices: none -> 45.8 us  [per_device(): lax.psum_scatter(partial.astype(jnp.bfloat16), 'zc', scatter_dimension=0,...]
    all_gather x1, waiting for transfers between devices: 84.7 us -> 44.6 us  [per_device(): piece = lax.all_gather(mixed, 'dp', axis=0, tiled=True)]
    all_gather x0 -> x1, blocking collectives: none -> 27.5 us  [per_device(): routes_g = lax.all_gather(routes[0], 'zc', axis=0, tiled=True)]
    dot_general x3 -> x6, matrix products: 12.5 us -> 31.8 us  [the longest x1 9.55 us: expert_rows(): lifted = jnp.dot(flat, w_expert_up, preferred_element_type=jnp.float32)]
    reduce_scatter x1, waiting for transfers between devices: 0.01 us -> 15.6 us  [per_device(): lax.psum_scatter(jnp.dot(hidden, w_shared_down, preferred_element_type=jn...]
    ppermute x0 -> x2, waiting for transfers between devices: none -> 14.5 us  [the longest x1 7.34 us: per_device(): from_partner = lax.ppermute(half_rows[slots:], 'core', swap)]
  transfers between devices with their start and end apart: 5 -> 9, of which waited for: 4 -> 8; matrix products, arithmetic and copies ran while one was open for 11% -> 12% of each run, Pallas kernels for 0% -> 0%
where the time goes in v1:
time: 441 us; the launch traced here: 434 us
  waiting for transfers between devices  194 us (44%)
  blocking collectives  88.4 us (20%)
  matrix products  82.1 us (19%)
  other arithmetic  30.5 us (7%)
  local copies, waits for them, and re-layouts  19.2 us (4%)
  between operations  14.2 us (3%)
  starting transfers between devices  5.47 us (1%)
    all_to_all x1, blocking collectives, per_device(): lax.all_to_all(send.reshape(dp_size, depth, width), 'dp', 0, 0, tiled=True)  51.4 us
    reduce_scatter x1, waiting for transfers between devices, per_device(): lax.psum_scatter(partial.astype(jnp.bfloat16), 'zc', scatter_dimension=0,...  45.8 us
    all_gather x1, waiting for transfers between devices, per_device(): piece = lax.all_gather(mixed, 'dp', axis=0, tiled=True)  44.6 us
    reduce_scatter x1, waiting for transfers between devices, per_device(): lax.psum_scatter(jnp.dot(attended, w_out, preferred_element_type=jnp.floa...  35.3 us
    all_gather x1, blocking collectives, per_device(): routes_g = lax.all_gather(routes[0], 'zc', axis=0, tiled=True)  27.5 us
    all_gather x1, waiting for transfers between devices, per_device(): lax.all_gather(normed, 'dp', axis=0, tiled=True)  26.3 us
    dot_general x1, matrix products, expert_rows(): jnp.dot(active, w_expert_down, preferred_element_type=jnp.float32)  19.7 us
    reduce_scatter x1, waiting for transfers between devices, per_device(): lax.psum_scatter(jnp.dot(hidden, w_shared_down, preferred_element_type=jn...  15.6 us
  transfers between devices with their start and end apart: 9, of which 8 were waited for; matrix products, arithmetic and copies ran while one was open for 12% of the time, Pallas kernels for 0%

profile of v1, /device:TPU:0, one launch (start us, length us, event | category | flops | bytes accessed | tf_op | source)
XLA Modules:
  0.0 434.2 jit_solution(3201670685680175112)
XLA Ops:
  10.0 9.5 %all-gather = s32[1,512]{1,0:T(1,128)S(1)} all-gather(s32[1,128]{1,0:T(1,128)} %param.17), channel_id=2, replica_groups=mesh['dp'=4,'zc'=4,'core'=2] {'dp'}, dimensions={1}, use_global_device_ids=true | all-gather | bytes 2560 | tf_op jit(solution)/shard_map/all_gather | solution.py:115
  21.7 26.3 %all-gather.6.cloned.1.call-done = bf16[512,2048]{1,0:T(8,128)(2,1)} async-done(((bf16[128,2048]{1,0:T(8,128)(2,1)}), bf16[512,2048]{1,0:T(8,128)(2,1)}) %all-gather.6.cloned.1.call-update) | async-done | bytes 2097168 | tf_op jit(solution)/shard_map/all_gather | solution.py:114
  48.0 2.5 convolution_bitcast_fusion
  51.1 3.5 fusion.73
  55.7 2.4 copy.44
  58.1 2.4 copy.43
  66.4 5.9 %fusion.15 = bf16[128,4,512]{2,0,1:T(8,128)(2,1)} fusion(f32[4,512]{1,0:T(4,128)S(1)} %fusion.3, f32[4,512]{1,0:T(4,128)S(1)} %get-tuple-element.34, f32[512,512,4]{1,0,2:T(8,128)} %copy-done.2, pred[512,512]{0,1:T(8,128)(4,1)S(1)} %compare_and_fusion.1, bf16[512,2048]{1,0:T(8,128)(2,1)} %all-gather.6.cloned.1.call-done, bf16[2048,128]{1,0:T(8,128)(2,1)} %param.22), kind=kOutput, calls=%fused_computation.38 | convolution fusion | flops 542441472 | bytes 7618560 | tf_op jit(solution)/shard_map/while/body/eval_jaxpr/kgqs,skd->qkgd/dot_general | solution.py:71
  72.3 4.4 %convolution_convert_fusion.3 = bf16[512,2048]{1,0:T(8,128)(2,1)} fusion(bf16[512,512]{0,1:T(8,128)(2,1)} %bitcast.109, bf16[512,2048]{1,0:T(8,128)(2,1)} %param.23), kind=kOutput, calls=%fused_computation.17 | convolution fusion | flops 1074790400 | bytes 4718592 | tf_op jit(solution)/shard_map/dot_general | solution.py:119
  76.8 35.3 %reduce-scatter.4.cloned.1.call-done = bf16[128,2048]{1,0:T(8,128)(2,1)} async-done(((bf16[512,2048]{1,0:T(8,128)(2,1)}), bf16[128,2048]{1,0:T(8,128)(2,1)}) %reduce-scatter.4.cloned.1.call-update) | async-done | bytes 524304 | tf_op jit(solution)/shard_map/reduce_scatter | solution.py:118
  113.4 2.1 fusion.21
  115.7 27.5 %all-gather.1 = s32[1,512,6]{2,1,0:T(8,128)} all-gather(s32[1,128,6]{2,1,0:T(8,128)S(1)} %copy.35), channel_id=3, replica_groups=mesh['dp'=4,'zc'=4,'core'=2] {'zc'}, dimensions={1}, use_global_device_ids=true | all-gather | bytes 15360 | tf_op jit(solution)/shard_map/all_gather | solution.py:144
  151.3 2.2 fusion
  153.4 12.1 %all-gather.10.cloned.1.call-done = bf16[512,2048]{1,0:T(8,128)(2,1)} async-done(((bf16[128,2048]{1,0:T(8,128)(2,1)}), bf16[512,2048]{1,0:T(8,128)(2,1)}) %all-gather.10.cloned.1.call-update) | async-done | bytes 2097168 | tf_op jit(solution)/shard_map/all_gather | solution.py:143
  165.6 4.1 convolution_convert_fusion.1
  169.7 51.4 %all_to_all.10 = bf16[4,256,2048]{2,1,0:T(8,128)(2,1)S(1)} all-to-all(bf16[4,256,2048]{2,1,0:T(8,128)(2,1)S(1)} %bitcast.104), channel_id=1, replica_groups=mesh['dp'=4,'zc'=4,'core'=2] {'dp'}, dimensions={0} | all-to-all | bytes 8388608 | tf_op jit(solution)/shard_map/all_to_all | solution.py:165
  221.1 7.2 %collective-permute-done = bf16[1024,2048]{1,0:T(8,128)(2,1)S(1)} collective-permute-done((bf16[1024,2048]{1,0:T(8,128)(2,1)S(1)}, bf16[1024,2048]{1,0:T(8,128)(2,1)S(1)}, u32[]{:S(2)}, u32[]{:S(2)}) %collective-permute-start) | collective-permute-done | bytes 4194336 | tf_op jit(solution)/shard_map/ppermute | solution.py:168
  230.2 9.5 %fusion.1 = f32[2048,704]{0,1:T(8,128)} fusion(bf16[2048,704]{0,1:T(8,128)(2,1)S(1)} %copy-done.12, bf16[1024,2048]{1,0:T(8,128)(2,1)S(1)} %collective-permute-done, bf16[1024,2048]{1,0:T(8,128)(2,1)S(1)} %bitcast.102), kind=kOutput, calls=%fused_computation.7 | convolution fusion | flops 5922357248 | bytes 17039360 | tf_op jit(solution)/shard_map/dot_general | solution.py:82
  239.8 19.7 %convolution_convert_fusion = bf16[2048,2048]{1,0:T(8,128)(2,1)} fusion(bf16[704,2048]{1,0:T(8,128)(2,1)S(1)} %copy-done, f32[2048,704]{0,1:T(8,128)} %fusion.1, bf16[2048,704]{0,1:T(8,128)(2,1)} %param.29, bf16[1024,2048]{1,0:T(8,128)(2,1)} %copy-done.11, bf16[1024,2048]{1,0:T(8,128)(2,1)} %bitcast.103), kind=kOutput, calls=%fused_computation.5 | convolution fusion | flops 11840782336 | bytes 28311552 | tf_op jit(solution)/shard_map/dot_general | solution.py:85
  259.5 4.7 %slice.38 = bf16[1024,2048]{1,0:T(8,128)(2,1)} slice(bf16[2048,2048]{1,0:T(8,128)(2,1)} %convolution_convert_fusion), slice={[1024:2048], [0:2048]} | slice | bytes 8388608 | tf_op jit(solution)/shard_map/slice | solution.py:172
  264.4 7.3 %collective-permute-done.1 = bf16[1024,2048]{1,0:T(8,128)(2,1)} collective-permute-done((bf16[1024,2048]{1,0:T(8,128)(2,1)}, bf16[1024,2048]{1,0:T(8,128)(2,1)}, u32[]{:S(2)}, u32[]{:S(2)}) %collective-permute-start.1) | collective-permute-done | bytes 4194336 | tf_op jit(solution)/shard_map/ppermute | solution.py:172
  271.7 7.7 %add_convert_fusion = bf16[1024,2048]{1,0:T(8,128)(2,1)} fusion(bf16[1024,2048]{1,0:T(8,128)(2,1)} %collective-permute-done.1, bf16[2048,2048]{1,0:T(8,128)(2,1)} %convolution_convert_fusion), kind=kLoop, calls=%fused_computation.4 | loop fusion | flops 8388608 | bytes 12582912 | tf_op jit(solution)/shard_map/convert_element_type | solution.py:175
  279.5 5.1 %all-to-all-start.1 = ((bf16[4,256,2048]{2,1,0:T(8,128)(2,1)}), bf16[4,256,2048]{2,1,0:T(8,128)(2,1)}, u32[]{:S(2)}, u32[]{:S(2)}) async-start(bf16[4,256,2048]{2,1,0:T(8,128)(2,1)} %bitcast.99), calls=%async_computation.3 | async-start | bytes 8388608 | tf_op jit(solution)/shard_map/all_to_all | solution.py:176
  284.6 44.6 %all-gather.8.cloned.1.call-done = bf16[512,2048]{1,0:T(8,128)(2,1)} async-done(((bf16[128,2048]{1,0:T(8,128)(2,1)}), bf16[512,2048]{1,0:T(8,128)(2,1)}) %all-gather.8.cloned.1.call-update) | async-done | bytes 2097168 | tf_op jit(solution)/shard_map/all_gather | solution.py:126
  329.3 4.4 %fusion.74 = f32[512,704]{0,1:T(8,128)} fusion(bf16[512,2048]{1,0:T(8,128)(2,1)} %all-gather.8.cloned.1.call-done, bf16[2048,704]{0,1:T(8,128)(2,1)S(1)} %copy-done.13), kind=kOutput, calls=%fused_computation.136 | convolution fusion | flops 1476395008 | bytes 6422528 | tf_op jit(solution)/shard_map/dot_general | solution.py:127
  333.7 8.7 %convolution_convert_fusion.2 = bf16[512,2048]{1,0:T(8,128)(2,1)} fusion(bf16[704,2048]{1,0:T(8,128)(2,1)} %param.28, bf16[512,2048]{1,0:T(8,128)(2,1)} %all-gather.8.cloned.1.call-done, bf16[2048,704]{0,1:T(8,128)(2,1)} %param.27, f32[512,704]{0,1:T(8,128)} %fusion.74), kind=kOutput, calls=%fused_computation.16 | convolution fusion | flops 2956001280 | bytes 11403264 | tf_op jit(solution)/shard_map/dot_general | solution.py:131
  343.3 2.1 select_reduce_fusion
  345.5 5.3 %fusion.10 = f32[512,2048]{1,0:T(8,128)S(1)} fusion(bf16[1024,2048]{1,0:T(8,128)(2,1)} %bitcast.20, f32[512,1024]{1,0:T(8,128)S(1)} %select_reduce_fusion), kind=kOutput, calls=%fused_computation.32 | convolution fusion | flops 2148007936 | bytes 10485760 | tf_op jit(solution)/shard_map/dot_general | solution.py:185
  350.8 4.5 %fusion.12 = f32[512,2048]{1,0:T(8,128)S(1)} fusion(bf16[1024,2048]{1,0:T(8,128)(2,1)} %bitcast.20, f32[512,1024]{1,0:T(8,128)S(1)} %select_reduce_fusion), kind=kOutput, calls=%fused_computation.34 | convolution fusion | flops 2149580800 | bytes 10485760 | tf_op jit(solution)/shard_map/dot_general | solution.py:186
  355.3 7.7 %add_convert_fusion.1 = bf16[512,2048]{1,0:T(8,128)(2,1)} fusion(f32[512,2048]{1,0:T(8,128)S(1)} %fusion.10, f32[512,2048]{1,0:T(8,128)S(1)} %fusion.12, bf16[1024,2048]{1,0:T(8,128)(2,1)} %bitcast.20, f32[512,1024]{1,0:T(8,128)} %copy-done.7), kind=kOutput, calls=%fused_computation.10 | convolution fusion | flops 2154299392 | bytes 16777216 | tf_op jit(solution)/shard_map/dot_general | solution.py:187
  363.0 15.6 %reduce-scatter.6.cloned.1.call-done = bf16[128,2048]{1,0:T(8,128)(2,1)} async-done(((bf16[512,2048]{1,0:T(8,128)(2,1)}), bf16[128,2048]{1,0:T(8,128)(2,1)}) %reduce-scatter.6.cloned.1.call-update) | async-done | bytes 524304 | tf_op jit(solution)/shard_map/reduce_scatter | solution.py:130
  378.6 45.8 %reduce-scatter.8.cloned.1.call-done = bf16[128,2048]{1,0:T(8,128)(2,1)} async-done(((bf16[512,2048]{1,0:T(8,128)(2,1)}), bf16[128,2048]{1,0:T(8,128)(2,1)}) %reduce-scatter.8.cloned.1.call-update) | async-done | bytes 524304 | tf_op jit(solution)/shard_map/reduce_scatter | solution.py:189
  424.4 2.5 fusion.28
  (81 shorter events, 25.8 us)
Async XLA Ops:
  6.5 233.2 %copy-start = (bf16[704,2048]{1,0:T(8,128)(2,1)S(1)}, bf16[704,2048]{1,0:T(8,128)(2,1)}, u32[]{:S(2)}) copy-start(bf16[704,2048]{1,0:T(8,128)(2,1)} %param.31) | copy-start | bytes 8650756
  6.5 41.5 %all-gather.6.cloned.1.call-start = ((), (), s32[]{:S(2)}) async-start(), calls=%async_computation.5 | async-start | bytes 2621440 | tf_op jit(solution)/shard_map/all_gather | solution.py:114
  10.0 102.1 %reduce-scatter.4.cloned.1.call-start = ((), (), s32[]{:S(2)}) async-start(), calls=%async_computation.6 | async-start | bytes 2621440 | tf_op jit(solution)/shard_map/reduce_scatter | solution.py:118
  63.6 1.9 copy-start.2
  72.3 39.8 %copy-start.3 = (bf16[1,128,2048]{2,1,0:T(8,128)(2,1)S(1)}, bf16[1,128,2048]{2,1,0:T(8,128)(2,1)}, u32[]{:S(2)}) copy-start(bf16[1,128,2048]{2,1,0:T(8,128)(2,1)} %param.16) | copy-start | bytes 1572868
  72.3 41.1 %copy-start.9 = (f32[2048]{0:T(1024)S(1)}, f32[2048]{0:T(1024)}, u32[]{:S(2)}) copy-start(f32[2048]{0:T(1024)} %param.24) | copy-start | bytes 24580
  72.3 43.3 %copy-start.10 = (s32[1,128,6]{1,0,2:T(1,128)S(1)}, s32[1,128,6]{1,0,2:T(1,128)}, u32[]{:S(2)}) copy-start(s32[1,128,6]{1,0,2:T(1,128)} %param.18) | copy-start | bytes 9220
  76.8 88.8 %all-gather.10.cloned.1.call-start = ((), (), s32[]{:S(2)}) async-start(), calls=%async_computation.9 | async-start | bytes 2621440 | tf_op jit(solution)/shard_map/all_gather | solution.py:143
  115.5 213.7 %all-gather.8.cloned.1.call-start = ((), (), s32[]{:S(2)}) async-start(), calls=%async_computation.7 | async-start | bytes 2621440 | tf_op jit(solution)/shard_map/all_gather | solution.py:126
  169.7 60.5 %copy-start.12 = (bf16[2048,704]{0,1:T(8,128)(2,1)S(1)}, bf16[2048,704]{0,1:T(8,128)(2,1)}, u32[]{:S(2)}) copy-start(bf16[2048,704]{0,1:T(8,128)(2,1)} %param.30) | copy-start | bytes 8650756
  221.1 7.2 %copy-start.5 = (bf16[4,256,2048]{2,1,0:T(8,128)(2,1)}, bf16[4,256,2048]{2,1,0:T(8,128)(2,1)S(1)}, u32[]{:S(2)}) copy-start(bf16[4,256,2048]{2,1,0:T(8,128)(2,1)S(1)} %all_to_all.10) | copy-start | bytes 12582916
  221.1 7.2 %collective-permute-start = (bf16[1024,2048]{1,0:T(8,128)(2,1)S(1)}, bf16[1024,2048]{1,0:T(8,128)(2,1)S(1)}, u32[]{:S(2)}, u32[]{:S(2)}) collective-permute-start(bf16[1024,2048]{1,0:T(8,128)(2,1)S(1)} %bitcast.101), channel_id=1, source_target_pairs={{0,1},{1,0},{2,3},{3,2},{4,5},{5,4},{6,7},{7,6},{8,9},{9,8},{10,11... | collective-permute-start | bytes 12582920 | tf_op jit(solution)/shard_map/ppermute | solution.py:168
  228.3 1.9 copy-start.11
  264.2 7.5 %collective-permute-start.1 = (bf16[1024,2048]{1,0:T(8,128)(2,1)}, bf16[1024,2048]{1,0:T(8,128)(2,1)}, u32[]{:S(2)}, u32[]{:S(2)}) collective-permute-start(bf16[1024,2048]{1,0:T(8,128)(2,1)} %slice.38), channel_id=1, source_target_pairs={{0,1},{1,0},{2,3},{3,2},{4,5},{5,4},{6,7},{7,6},{8,9},{9,8},{10,11... | collective-permute-start | bytes 12582920 | tf_op jit(solution)/shard_map/ppermute | solution.py:172
  279.5 49.8 %copy-start.13 = (bf16[2048,704]{0,1:T(8,128)(2,1)S(1)}, bf16[2048,704]{0,1:T(8,128)(2,1)}, u32[]{:S(2)}) copy-start(bf16[2048,704]{0,1:T(8,128)(2,1)} %param.26) | copy-start | bytes 8650756
  279.5 66.0 %all-to-all-start.1 = ((bf16[4,256,2048]{2,1,0:T(8,128)(2,1)}), bf16[4,256,2048]{2,1,0:T(8,128)(2,1)}, u32[]{:S(2)}, u32[]{:S(2)}) async-start(bf16[4,256,2048]{2,1,0:T(8,128)(2,1)} %bitcast.99), calls=%async_computation.3 | async-start | bytes 8388608 | tf_op jit(solution)/shard_map/all_to_all | solution.py:176
  284.6 94.0 %reduce-scatter.6.cloned.1.call-start = ((), (), s32[]{:S(2)}) async-start(), calls=%async_computation.8 | async-start | bytes 2621440 | tf_op jit(solution)/shard_map/reduce_scatter | solution.py:130
  333.7 8.7 %copy-start.4 = (s32[1,512,6]{2,1,0:T(8,128)S(1)}, s32[1,512,6]{2,1,0:T(8,128)}, u32[]{:S(2)}) copy-start(s32[1,512,6]{2,1,0:T(8,128)} %all-gather.1) | copy-start | bytes 36868
  333.7 8.9 %copy-start.6 = (bf16[512,2048]{1,0:T(8,128)(2,1)S(1)}, bf16[512,2048]{1,0:T(8,128)(2,1)}, u32[]{:S(2)}) copy-start(bf16[512,2048]{1,0:T(8,128)(2,1)} %all-gather.10.cloned.1.call-done) | copy-start | bytes 6291460
  333.7 8.9 %copy-start.8 = (bf16[2048,16]{0,1:T(8,128)(2,1)S(1)}, bf16[2048,16]{0,1:T(8,128)(2,1)}, u32[]{:S(2)}) copy-start(bf16[2048,16]{0,1:T(8,128)(2,1)} %param.25) | copy-start | bytes 196612
  342.4 82.0 %reduce-scatter.8.cloned.1.call-start = ((), (), s32[]{:S(2)}) async-start(), calls=%async_computation.10 | async-start | bytes 2621440 | tf_op jit(solution)/shard_map/reduce_scatter | solution.py:189
  345.5 5.3 %copy-start.7 = (f32[512,1024]{1,0:T(8,128)}, f32[512,1024]{1,0:T(8,128)S(1)}, u32[]{:S(2)}) copy-start(f32[512,1024]{1,0:T(8,128)S(1)} %select_reduce_fusion) | copy-start | bytes 6291460
  355.3 71.6 %copy-start.1 = (bf16[704,2048]{1,0:T(8,128)(2,1)S(1)}, bf16[704,2048]{1,0:T(8,128)(2,1)}, u32[]{:S(2)}) copy-start(bf16[704,2048]{1,0:T(8,128)(2,1)} %param.31) | copy-start | bytes 8650756
Sparse Core Ops, SparseCore 0:
  10.1 37.8 all-gather.5
  76.9 35.1 reduce-scatter.3
  115.7 49.8 all-gather.9
  264.5 64.7 all-gather.7
  342.5 36.0 reduce-scatter.5
  380.7 43.6 reduce-scatter.7
